TPU v7x, 512 devices: a whole 4x4x16 slice. The times are simulated.
512 devices in a mesh: pipe: 16 (over z), seq: 8 (over y, core), dp: 4 (over x).
Axes of the slice: x: 4, y: 4, z: 16, core: 2. Of those that a mesh axis runs over, the one named last changes fastest.
Arguments:
- acts: bfloat16 [16, 4, 1024, 8192], P('pipe', 'dp', 'seq'), may hold values from -6 to 6
- top_grad: bfloat16 [4, 1024, 8192], P('dp', 'seq'), may hold values from -6 to 6
- a_rows: bfloat16 [16, 32, 8192], P('pipe', None, ('seq', 'dp')), may hold values from -1 to 1
- b_rows: bfloat16 [16, 32, 8192], P('pipe', None, ('seq', 'dp')), may hold values from -0.375 to 0.375
- gain: bfloat16 [16, 8192], P('pipe', ('seq', 'dp')), may hold values from 0.5 to 1.5
Outputs:
- grad_a: float32 [16, 32, 8192], P('pipe', None, ('seq', 'dp'))
- grad_b: float32 [16, 32, 8192], P('pipe', None, ('seq', 'dp'))
- grad_gain: float32 [16, 8192], P('pipe', ('seq', 'dp'))
- clip_factors: float32 [4], P('dp')
All inputs are finite; a program needn't handle non-finite values.
Results may differ from a plain program's by a relative error of at most 0.019.
Values may be sent and summed in bfloat16 or wider, within the bound.
No kernel may reach another device: no remote copies, remote signals or barrier semaphores. Data moves between devices by JAX's collectives and lax.ppermute only.
A program may use at most 64 MiB of HBM per device.

v0:
```python
import math
import jax
import jax.numpy as jnp
from jax import lax
from jax.sharding import PartitionSpec as P

rows_per_block = 16


def from_behind(value, axis, steps):
    count = lax.axis_size(axis)
    initial, last = (max(0, -steps), min(count, count - steps))
    return lax.ppermute(value, axis, [(source, source + steps) for source in range(initial, last)])


def on_device(acts, top_grad, a_rows, b_rows, gain):
    sections = lax.axis_size("pipe")
    section = lax.axis_index("pipe")
    hidden = acts[0, 0]
    top = top_grad[0]
    rank = a_rows.shape[1]
    params = jnp.concatenate([a_rows[0], b_rows[0], gain], axis=0)
    whole = lax.all_gather(params, ("seq", "dp"), axis=1, tiled=True)
    a_full = whole[:rank]
    b_full = whole[rank : 2 * rank]
    gain_float = whole[2 * rank].astype(jnp.float32)
    rows, width = hidden.shape
    block_total = rows // rows_per_block
    hidden_float = hidden.astype(jnp.float32)
    inverse_root_mean = jnp.sqrt(
        jnp.mean(hidden_float * hidden_float, axis=-1, keepdims=True) + 1e-05
    )
    input_normalized = hidden_float / inverse_root_mean
    normalized_rows = (input_normalized * gain_float).astype(jnp.bfloat16)
    low = jnp.dot(normalized_rows, a_full.T, preferred_element_type=jnp.float32).astype(
        jnp.bfloat16
    )
    contract_last = (((1,), (1,)), ((), ()))
    contract_first = (((0,), (0,)), ((), ()))

    def back_block(upstream_gradient, block_offset):
        hidden_part = lax.dynamic_slice_in_dim(hidden, block_offset, rows_per_block, 0)
        r_part = lax.dynamic_slice_in_dim(inverse_root_mean, block_offset, rows_per_block, 0)
        input_portion = hidden_part.astype(jnp.float32) / r_part
        d_low = lax.dot_general(
            upstream_gradient, b_full, contract_last, preferred_element_type=jnp.float32
        ).astype(jnp.bfloat16)
        normalized_gradient = jnp.dot(d_low, a_full, preferred_element_type=jnp.float32)
        input_gradient = normalized_gradient * gain_float
        hidden_gradient = (
            upstream_gradient.astype(jnp.float32)
            + (
                input_gradient
                - input_portion * jnp.mean(input_gradient * input_portion, axis=-1, keepdims=True)
            )
            / r_part
        )
        return hidden_gradient.astype(jnp.bfloat16)

    def turn(turn_index, carry):
        incoming, store = carry
        block_index = turn_index - (sections - 1 - section)
        inside = jnp.logical_and(block_index >= 0, block_index < block_total)
        block_offset = jnp.clip(block_index, 0, block_total - 1) * rows_per_block
        top_block = lax.dynamic_slice_in_dim(top, block_offset, rows_per_block, 0)
        source = jnp.where(section == sections - 1, top_block, incoming)
        slot = jnp.where(inside, block_index, block_total)
        store = lax.dynamic_update_slice_in_dim(store, source[None], slot, 0)
        result = back_block(source, block_offset)
        incoming = from_behind(result, "pipe", -1)
        return (incoming, store)

    begin = (
        jnp.zeros((rows_per_block, width), jnp.bfloat16),
        jnp.zeros((block_total + 1, rows_per_block, width), jnp.bfloat16),
    )
    store = lax.fori_loop(0, sections + block_total - 1, turn, begin)[1]
    mine = store[:block_total].reshape(rows, width)
    d_low = lax.dot_general(mine, b_full, contract_last, preferred_element_type=jnp.float32).astype(
        jnp.bfloat16
    )
    normalized_gradient = jnp.dot(d_low, a_full, preferred_element_type=jnp.float32)
    grad_a = lax.dot_general(
        d_low, normalized_rows, contract_first, preferred_element_type=jnp.float32
    )
    grad_b = lax.dot_general(low, mine, contract_first, preferred_element_type=jnp.float32)
    gain_gradient = jnp.sum(normalized_gradient * input_normalized, axis=0)[None, :]
    grads = jnp.concatenate([grad_a, grad_b, gain_gradient], axis=0)
    part = lax.psum_scatter(grads, "seq", scatter_dimension=1, tiled=True)
    examples = lax.axis_size("dp")
    example = lax.axis_index("dp")
    square = jnp.sum(part * part)
    squares = jnp.where(jnp.arange(examples) == example, square, 0.0).astype(jnp.float32)
    totals = lax.psum(squares, ("pipe", "seq", "dp"))
    bound = math.sqrt(sections * (2 * rank + 1) * width)
    factors = bound / (jnp.sqrt(totals) + 0.01 * bound)
    gathered = lax.all_gather(part, "dp", axis=0, tiled=False)
    share = part.shape[1] // examples
    pieces = lax.dynamic_slice_in_dim(gathered, example * share, share, 2)
    combined = jnp.sum(factors[:, None, None] * pieces, axis=0)
    out_a = combined[:rank]
    out_b = combined[rank : 2 * rank]
    out_g = combined[2 * rank :]
    factor = lax.dynamic_slice_in_dim(factors, example, 1, 0)
    return (out_a[None], out_b[None], out_g, factor)


def solution(mesh):
    in_specs = (
        P("pipe", "dp", "seq", None),
        P("dp", "seq", None),
        P("pipe", None, ("seq", "dp")),
        P("pipe", None, ("seq", "dp")),
        P("pipe", ("seq", "dp")),
    )
    out_specs = (
        P("pipe", None, ("seq", "dp")),
        P("pipe", None, ("seq", "dp")),
        P("pipe", ("seq", "dp")),
        P("dp"),
    )
    return jax.shard_map(
        on_device, mesh=mesh, in_specs=in_specs, out_specs=out_specs, check_vma=False
    )
```

profile of v0, /device:TPU:1, one launch (start us, length us, event | category | flops | bytes accessed | tf_op | source)
XLA Modules:
  0.0 594.1 jit_solution(15978239011922078406)
XLA Ops:
  10.8 64.3 %all-gather.5.cloned.1.call-done = bf16[65,8192]{1,0:T(8,128)(2,1)} async-done(((bf16[65,256]{1,0:T(8,128)(2,1)}), bf16[65,8192]{1,0:T(8,128)(2,1)}) %all-gather.5.cloned.1.call-update) | async-done | bytes 1064976 | tf_op jit(solution)/shard_map/all_gather | solution.py:23
  78.5 318.4 %while.17 = (s32[]{:T(128)}, bf16[16,8192]{1,0:T(8,128)(2,1)S(1)}, bf16[9,16,8192]{2,1,0:T(8,128)(2,1)S(1)}, pred[]{:T(512)}, s32[]{:T(128)}, /*index=5*/bf16[12...) while((s32[]{:T(128)}, bf16[16,8192]{1,0:T(8,128)(2,1)S(1)}, ...), condition=%wide.region_3.4_spmd, body=%wide.region_1.3_spmd.sunk | while | flops 18612752 | bytes 5538680 | solution.py:77
  84.7 8.4 %collective-permute-done = bf16[16,8192]{1,0:T(8,128)(2,1)S(1)} collective-permute-done((bf16[16,8192]{1,0:T(8,128)(2,1)}, bf16[16,8192]{1,0:T(8,128)(2,1)S(1)}, u32[]{:S(2)}, u32[]{:S(2)}) %collective-permute-start) | collective-permute-done | bytes 262176 | tf_op jit(solution)/shard_map/while/body/eval_jaxpr/ppermute | solution.py:13
  99.3 7.5 %collective-permute-done = bf16[16,8192]{1,0:T(8,128)(2,1)S(1)} collective-permute-done((bf16[16,8192]{1,0:T(8,128)(2,1)}, bf16[16,8192]{1,0:T(8,128)(2,1)S(1)}, u32[]{:S(2)}, u32[]{:S(2)}) %collective-permute-start) | collective-permute-done | bytes 262176 | tf_op jit(solution)/shard_map/while/body/eval_jaxpr/ppermute | solution.py:13
  113.0 6.7 %collective-permute-done = bf16[16,8192]{1,0:T(8,128)(2,1)S(1)} collective-permute-done((bf16[16,8192]{1,0:T(8,128)(2,1)}, bf16[16,8192]{1,0:T(8,128)(2,1)S(1)}, u32[]{:S(2)}, u32[]{:S(2)}) %collective-permute-start) | collective-permute-done | bytes 262176 | tf_op jit(solution)/shard_map/while/body/eval_jaxpr/ppermute | solution.py:13
  125.9 8.2 %collective-permute-done = bf16[16,8192]{1,0:T(8,128)(2,1)S(1)} collective-permute-done((bf16[16,8192]{1,0:T(8,128)(2,1)}, bf16[16,8192]{1,0:T(8,128)(2,1)S(1)}, u32[]{:S(2)}, u32[]{:S(2)}) %collective-permute-start) | collective-permute-done | bytes 262176 | tf_op jit(solution)/shard_map/while/body/eval_jaxpr/ppermute | solution.py:13
  165.7 7.2 %collective-permute-done = bf16[16,8192]{1,0:T(8,128)(2,1)S(1)} collective-permute-done((bf16[16,8192]{1,0:T(8,128)(2,1)}, bf16[16,8192]{1,0:T(8,128)(2,1)S(1)}, u32[]{:S(2)}, u32[]{:S(2)}) %collective-permute-start) | collective-permute-done | bytes 262176 | tf_op jit(solution)/shard_map/while/body/eval_jaxpr/ppermute | solution.py:13
  179.1 7.2 %collective-permute-done = bf16[16,8192]{1,0:T(8,128)(2,1)S(1)} collective-permute-done((bf16[16,8192]{1,0:T(8,128)(2,1)}, bf16[16,8192]{1,0:T(8,128)(2,1)S(1)}, u32[]{:S(2)}, u32[]{:S(2)}) %collective-permute-start) | collective-permute-done | bytes 262176 | tf_op jit(solution)/shard_map/while/body/eval_jaxpr/ppermute | solution.py:13
  192.5 7.2 %collective-permute-done = bf16[16,8192]{1,0:T(8,128)(2,1)S(1)} collective-permute-done((bf16[16,8192]{1,0:T(8,128)(2,1)}, bf16[16,8192]{1,0:T(8,128)(2,1)S(1)}, u32[]{:S(2)}, u32[]{:S(2)}) %collective-permute-start) | collective-permute-done | bytes 262176 | tf_op jit(solution)/shard_map/while/body/eval_jaxpr/ppermute | solution.py:13
  206.0 7.2 %collective-permute-done = bf16[16,8192]{1,0:T(8,128)(2,1)S(1)} collective-permute-done((bf16[16,8192]{1,0:T(8,128)(2,1)}, bf16[16,8192]{1,0:T(8,128)(2,1)S(1)}, u32[]{:S(2)}, u32[]{:S(2)}) %collective-permute-start) | collective-permute-done | bytes 262176 | tf_op jit(solution)/shard_map/while/body/eval_jaxpr/ppermute | solution.py:13
  219.4 7.2 %collective-permute-done = bf16[16,8192]{1,0:T(8,128)(2,1)S(1)} collective-permute-done((bf16[16,8192]{1,0:T(8,128)(2,1)}, bf16[16,8192]{1,0:T(8,128)(2,1)S(1)}, u32[]{:S(2)}, u32[]{:S(2)}) %collective-permute-start) | collective-permute-done | bytes 262176 | tf_op jit(solution)/shard_map/while/body/eval_jaxpr/ppermute | solution.py:13
  232.8 7.2 %collective-permute-done = bf16[16,8192]{1,0:T(8,128)(2,1)S(1)} collective-permute-done((bf16[16,8192]{1,0:T(8,128)(2,1)}, bf16[16,8192]{1,0:T(8,128)(2,1)S(1)}, u32[]{:S(2)}, u32[]{:S(2)}) %collective-permute-start) | collective-permute-done | bytes 262176 | tf_op jit(solution)/shard_map/while/body/eval_jaxpr/ppermute | solution.py:13
  246.3 8.4 %collective-permute-done = bf16[16,8192]{1,0:T(8,128)(2,1)S(1)} collective-permute-done((bf16[16,8192]{1,0:T(8,128)(2,1)}, bf16[16,8192]{1,0:T(8,128)(2,1)S(1)}, u32[]{:S(2)}, u32[]{:S(2)}) %collective-permute-start) | collective-permute-done | bytes 262176 | tf_op jit(solution)/shard_map/while/body/eval_jaxpr/ppermute | solution.py:13
  260.9 10.0 %collective-permute-done = bf16[16,8192]{1,0:T(8,128)(2,1)S(1)} collective-permute-done((bf16[16,8192]{1,0:T(8,128)(2,1)}, bf16[16,8192]{1,0:T(8,128)(2,1)S(1)}, u32[]{:S(2)}, u32[]{:S(2)}) %collective-permute-start) | collective-permute-done | bytes 262176 | tf_op jit(solution)/shard_map/while/body/eval_jaxpr/ppermute | solution.py:13
  277.1 10.7 %collective-permute-done = bf16[16,8192]{1,0:T(8,128)(2,1)S(1)} collective-permute-done((bf16[16,8192]{1,0:T(8,128)(2,1)}, bf16[16,8192]{1,0:T(8,128)(2,1)S(1)}, u32[]{:S(2)}, u32[]{:S(2)}) %collective-permute-start) | collective-permute-done | bytes 262176 | tf_op jit(solution)/shard_map/while/body/eval_jaxpr/ppermute | solution.py:13
  294.0 9.9 %collective-permute-done = bf16[16,8192]{1,0:T(8,128)(2,1)S(1)} collective-permute-done((bf16[16,8192]{1,0:T(8,128)(2,1)}, bf16[16,8192]{1,0:T(8,128)(2,1)S(1)}, u32[]{:S(2)}, u32[]{:S(2)}) %collective-permute-start) | collective-permute-done | bytes 262176 | tf_op jit(solution)/shard_map/while/body/eval_jaxpr/ppermute | solution.py:13
  310.1 7.9 %collective-permute-done = bf16[16,8192]{1,0:T(8,128)(2,1)S(1)} collective-permute-done((bf16[16,8192]{1,0:T(8,128)(2,1)}, bf16[16,8192]{1,0:T(8,128)(2,1)S(1)}, u32[]{:S(2)}, u32[]{:S(2)}) %collective-permute-start) | collective-permute-done | bytes 262176 | tf_op jit(solution)/shard_map/while/body/eval_jaxpr/ppermute | solution.py:13
  324.2 6.7 %collective-permute-done = bf16[16,8192]{1,0:T(8,128)(2,1)S(1)} collective-permute-done((bf16[16,8192]{1,0:T(8,128)(2,1)}, bf16[16,8192]{1,0:T(8,128)(2,1)S(1)}, u32[]{:S(2)}, u32[]{:S(2)}) %collective-permute-start) | collective-permute-done | bytes 262176 | tf_op jit(solution)/shard_map/while/body/eval_jaxpr/ppermute | solution.py:13
  349.6 7.0 %collective-permute-done = bf16[16,8192]{1,0:T(8,128)(2,1)S(1)} collective-permute-done((bf16[16,8192]{1,0:T(8,128)(2,1)}, bf16[16,8192]{1,0:T(8,128)(2,1)S(1)}, u32[]{:S(2)}, u32[]{:S(2)}) %collective-permute-start) | collective-permute-done | bytes 262176 | tf_op jit(solution)/shard_map/while/body/eval_jaxpr/ppermute | solution.py:13
  362.8 7.2 %collective-permute-done = bf16[16,8192]{1,0:T(8,128)(2,1)S(1)} collective-permute-done((bf16[16,8192]{1,0:T(8,128)(2,1)}, bf16[16,8192]{1,0:T(8,128)(2,1)S(1)}, u32[]{:S(2)}, u32[]{:S(2)}) %collective-permute-start) | collective-permute-done | bytes 262176 | tf_op jit(solution)/shard_map/while/body/eval_jaxpr/ppermute | solution.py:13
  376.2 7.2 %collective-permute-done = bf16[16,8192]{1,0:T(8,128)(2,1)S(1)} collective-permute-done((bf16[16,8192]{1,0:T(8,128)(2,1)}, bf16[16,8192]{1,0:T(8,128)(2,1)S(1)}, u32[]{:S(2)}, u32[]{:S(2)}) %collective-permute-start) | collective-permute-done | bytes 262176 | tf_op jit(solution)/shard_map/while/body/eval_jaxpr/ppermute | solution.py:13
  389.7 7.2 %collective-permute-done = bf16[16,8192]{1,0:T(8,128)(2,1)S(1)} collective-permute-done((bf16[16,8192]{1,0:T(8,128)(2,1)}, bf16[16,8192]{1,0:T(8,128)(2,1)S(1)}, u32[]{:S(2)}, u32[]{:S(2)}) %collective-permute-start) | collective-permute-done | bytes 262176 | tf_op jit(solution)/shard_map/while/body/eval_jaxpr/ppermute | solution.py:13
  410.6 65.9 %reduce-scatter.2.cloned.1.call-done = f32[65,1024]{1,0:T(8,128)} async-done(((f32[65,8192]{1,0:T(8,128)}), f32[65,1024]{1,0:T(8,128)}) %reduce-scatter.2.cloned.1.call-update) | async-done | bytes 266256 | tf_op jit(solution)/shard_map/reduce_scatter | solution.py:89
  478.8 106.0 %psum.7 = f32[4]{0:T(128)S(1)} all-reduce(f32[4]{0:T(128)S(1)} %compare_select_fusion), channel_id=1, replica_groups=mesh['pipe'=16,'seq'=8,'dp'=4] {'pipe','seq','dp'}, use_global_device_ids=true, to_apply=%region_7.8 | all-reduce | flops 4 | bytes 32 | tf_op jit(solution)/shard_map/psum | solution.py:94
  (184 shorter events, 187.3 us)
Async XLA Ops:
  7.2 67.9 %all-gather.5.cloned.1.call-start = ((), (), s32[]{:S(2)}) async-start(), calls=%async_computation.1 | async-start | bytes 1216512 | tf_op jit(solution)/shard_map/all_gather | solution.py:23
  8.6 467.8 %reduce-scatter.2.cloned.1.call-start = ((), (), s32[]{:S(2)}) async-start(), calls=%async_computation.2 | async-start | bytes 2654208 | tf_op jit(solution)/shard_map/reduce_scatter | solution.py:89
  83.4 9.7 %collective-permute-start = (bf16[16,8192]{1,0:T(8,128)(2,1)}, bf16[16,8192]{1,0:T(8,128)(2,1)S(1)}, u32[]{:S(2)}, u32[]{:S(2)}) collective-permute-start(bf16[16,8192]{1,0:T(8,128)(2,1)} %add_convert_fusion.2), channel_id=1, source_target_pairs={{32,0},{64,32},{96,64},{128,96},{160,128},{192,160},{224,192},{256... | collective-permute-start | bytes 786440 | tf_op jit(solution)/shard_map/while/body/eval_jaxpr/ppermute | solution.py:13
  98.0 8.8 %collective-permute-start = (bf16[16,8192]{1,0:T(8,128)(2,1)}, bf16[16,8192]{1,0:T(8,128)(2,1)S(1)}, u32[]{:S(2)}, u32[]{:S(2)}) collective-permute-start(bf16[16,8192]{1,0:T(8,128)(2,1)} %add_convert_fusion.2), channel_id=1, source_target_pairs={{32,0},{64,32},{96,64},{128,96},{160,128},{192,160},{224,192},{256... | collective-permute-start | bytes 786440 | tf_op jit(solution)/shard_map/while/body/eval_jaxpr/ppermute | solution.py:13
  111.7 8.0 %collective-permute-start = (bf16[16,8192]{1,0:T(8,128)(2,1)}, bf16[16,8192]{1,0:T(8,128)(2,1)S(1)}, u32[]{:S(2)}, u32[]{:S(2)}) collective-permute-start(bf16[16,8192]{1,0:T(8,128)(2,1)} %add_convert_fusion.2), channel_id=1, source_target_pairs={{32,0},{64,32},{96,64},{128,96},{160,128},{192,160},{224,192},{256... | collective-permute-start | bytes 786440 | tf_op jit(solution)/shard_map/while/body/eval_jaxpr/ppermute | solution.py:13
  124.6 9.5 %collective-permute-start = (bf16[16,8192]{1,0:T(8,128)(2,1)}, bf16[16,8192]{1,0:T(8,128)(2,1)S(1)}, u32[]{:S(2)}, u32[]{:S(2)}) collective-permute-start(bf16[16,8192]{1,0:T(8,128)(2,1)} %add_convert_fusion.2), channel_id=1, source_target_pairs={{32,0},{64,32},{96,64},{128,96},{160,128},{192,160},{224,192},{256... | collective-permute-start | bytes 786440 | tf_op jit(solution)/shard_map/while/body/eval_jaxpr/ppermute | solution.py:13
  151.6 7.9 %collective-permute-start = (bf16[16,8192]{1,0:T(8,128)(2,1)}, bf16[16,8192]{1,0:T(8,128)(2,1)S(1)}, u32[]{:S(2)}, u32[]{:S(2)}) collective-permute-start(bf16[16,8192]{1,0:T(8,128)(2,1)} %add_convert_fusion.2), channel_id=1, source_target_pairs={{32,0},{64,32},{96,64},{128,96},{160,128},{192,160},{224,192},{256... | collective-permute-start | bytes 786440 | tf_op jit(solution)/shard_map/while/body/eval_jaxpr/ppermute | solution.py:13
  164.4 8.5 %collective-permute-start = (bf16[16,8192]{1,0:T(8,128)(2,1)}, bf16[16,8192]{1,0:T(8,128)(2,1)S(1)}, u32[]{:S(2)}, u32[]{:S(2)}) collective-permute-start(bf16[16,8192]{1,0:T(8,128)(2,1)} %add_convert_fusion.2), channel_id=1, source_target_pairs={{32,0},{64,32},{96,64},{128,96},{160,128},{192,160},{224,192},{256... | collective-permute-start | bytes 786440 | tf_op jit(solution)/shard_map/while/body/eval_jaxpr/ppermute | solution.py:13
  177.8 8.5 %collective-permute-start = (bf16[16,8192]{1,0:T(8,128)(2,1)}, bf16[16,8192]{1,0:T(8,128)(2,1)S(1)}, u32[]{:S(2)}, u32[]{:S(2)}) collective-permute-start(bf16[16,8192]{1,0:T(8,128)(2,1)} %add_convert_fusion.2), channel_id=1, source_target_pairs={{32,0},{64,32},{96,64},{128,96},{160,128},{192,160},{224,192},{256... | collective-permute-start | bytes 786440 | tf_op jit(solution)/shard_map/while/body/eval_jaxpr/ppermute | solution.py:13
  191.2 8.5 %collective-permute-start = (bf16[16,8192]{1,0:T(8,128)(2,1)}, bf16[16,8192]{1,0:T(8,128)(2,1)S(1)}, u32[]{:S(2)}, u32[]{:S(2)}) collective-permute-start(bf16[16,8192]{1,0:T(8,128)(2,1)} %add_convert_fusion.2), channel_id=1, source_target_pairs={{32,0},{64,32},{96,64},{128,96},{160,128},{192,160},{224,192},{256... | collective-permute-start | bytes 786440 | tf_op jit(solution)/shard_map/while/body/eval_jaxpr/ppermute | solution.py:13
  204.7 8.5 %collective-permute-start = (bf16[16,8192]{1,0:T(8,128)(2,1)}, bf16[16,8192]{1,0:T(8,128)(2,1)S(1)}, u32[]{:S(2)}, u32[]{:S(2)}) collective-permute-start(bf16[16,8192]{1,0:T(8,128)(2,1)} %add_convert_fusion.2), channel_id=1, source_target_pairs={{32,0},{64,32},{96,64},{128,96},{160,128},{192,160},{224,192},{256... | collective-permute-start | bytes 786440 | tf_op jit(solution)/shard_map/while/body/eval_jaxpr/ppermute | solution.py:13
  218.1 8.5 %collective-permute-start = (bf16[16,8192]{1,0:T(8,128)(2,1)}, bf16[16,8192]{1,0:T(8,128)(2,1)S(1)}, u32[]{:S(2)}, u32[]{:S(2)}) collective-permute-start(bf16[16,8192]{1,0:T(8,128)(2,1)} %add_convert_fusion.2), channel_id=1, source_target_pairs={{32,0},{64,32},{96,64},{128,96},{160,128},{192,160},{224,192},{256... | collective-permute-start | bytes 786440 | tf_op jit(solution)/shard_map/while/body/eval_jaxpr/ppermute | solution.py:13
  231.6 8.5 %collective-permute-start = (bf16[16,8192]{1,0:T(8,128)(2,1)}, bf16[16,8192]{1,0:T(8,128)(2,1)S(1)}, u32[]{:S(2)}, u32[]{:S(2)}) collective-permute-start(bf16[16,8192]{1,0:T(8,128)(2,1)} %add_convert_fusion.2), channel_id=1, source_target_pairs={{32,0},{64,32},{96,64},{128,96},{160,128},{192,160},{224,192},{256... | collective-permute-start | bytes 786440 | tf_op jit(solution)/shard_map/while/body/eval_jaxpr/ppermute | solution.py:13
  245.0 9.7 %collective-permute-start = (bf16[16,8192]{1,0:T(8,128)(2,1)}, bf16[16,8192]{1,0:T(8,128)(2,1)S(1)}, u32[]{:S(2)}, u32[]{:S(2)}) collective-permute-start(bf16[16,8192]{1,0:T(8,128)(2,1)} %add_convert_fusion.2), channel_id=1, source_target_pairs={{32,0},{64,32},{96,64},{128,96},{160,128},{192,160},{224,192},{256... | collective-permute-start | bytes 786440 | tf_op jit(solution)/shard_map/while/body/eval_jaxpr/ppermute | solution.py:13
  259.6 11.3 %collective-permute-start = (bf16[16,8192]{1,0:T(8,128)(2,1)}, bf16[16,8192]{1,0:T(8,128)(2,1)S(1)}, u32[]{:S(2)}, u32[]{:S(2)}) collective-permute-start(bf16[16,8192]{1,0:T(8,128)(2,1)} %add_convert_fusion.2), channel_id=1, source_target_pairs={{32,0},{64,32},{96,64},{128,96},{160,128},{192,160},{224,192},{256... | collective-permute-start | bytes 786440 | tf_op jit(solution)/shard_map/while/body/eval_jaxpr/ppermute | solution.py:13
  275.8 11.9 %collective-permute-start = (bf16[16,8192]{1,0:T(8,128)(2,1)}, bf16[16,8192]{1,0:T(8,128)(2,1)S(1)}, u32[]{:S(2)}, u32[]{:S(2)}) collective-permute-start(bf16[16,8192]{1,0:T(8,128)(2,1)} %add_convert_fusion.2), channel_id=1, source_target_pairs={{32,0},{64,32},{96,64},{128,96},{160,128},{192,160},{224,192},{256... | collective-permute-start | bytes 786440 | tf_op jit(solution)/shard_map/while/body/eval_jaxpr/ppermute | solution.py:13
  292.7 11.2 %collective-permute-start = (bf16[16,8192]{1,0:T(8,128)(2,1)}, bf16[16,8192]{1,0:T(8,128)(2,1)S(1)}, u32[]{:S(2)}, u32[]{:S(2)}) collective-permute-start(bf16[16,8192]{1,0:T(8,128)(2,1)} %add_convert_fusion.2), channel_id=1, source_target_pairs={{32,0},{64,32},{96,64},{128,96},{160,128},{192,160},{224,192},{256... | collective-permute-start | bytes 786440 | tf_op jit(solution)/shard_map/while/body/eval_jaxpr/ppermute | solution.py:13
  308.8 9.2 %collective-permute-start = (bf16[16,8192]{1,0:T(8,128)(2,1)}, bf16[16,8192]{1,0:T(8,128)(2,1)S(1)}, u32[]{:S(2)}, u32[]{:S(2)}) collective-permute-start(bf16[16,8192]{1,0:T(8,128)(2,1)} %add_convert_fusion.2), channel_id=1, source_target_pairs={{32,0},{64,32},{96,64},{128,96},{160,128},{192,160},{224,192},{256... | collective-permute-start | bytes 786440 | tf_op jit(solution)/shard_map/while/body/eval_jaxpr/ppermute | solution.py:13
  322.9 8.0 %collective-permute-start = (bf16[16,8192]{1,0:T(8,128)(2,1)}, bf16[16,8192]{1,0:T(8,128)(2,1)S(1)}, u32[]{:S(2)}, u32[]{:S(2)}) collective-permute-start(bf16[16,8192]{1,0:T(8,128)(2,1)} %add_convert_fusion.2), channel_id=1, source_target_pairs={{32,0},{64,32},{96,64},{128,96},{160,128},{192,160},{224,192},{256... | collective-permute-start | bytes 786440 | tf_op jit(solution)/shard_map/while/body/eval_jaxpr/ppermute | solution.py:13
  348.4 8.2 %collective-permute-start = (bf16[16,8192]{1,0:T(8,128)(2,1)}, bf16[16,8192]{1,0:T(8,128)(2,1)S(1)}, u32[]{:S(2)}, u32[]{:S(2)}) collective-permute-start(bf16[16,8192]{1,0:T(8,128)(2,1)} %add_convert_fusion.2), channel_id=1, source_target_pairs={{32,0},{64,32},{96,64},{128,96},{160,128},{192,160},{224,192},{256... | collective-permute-start | bytes 786440 | tf_op jit(solution)/shard_map/while/body/eval_jaxpr/ppermute | solution.py:13
  361.5 8.5 %collective-permute-start = (bf16[16,8192]{1,0:T(8,128)(2,1)}, bf16[16,8192]{1,0:T(8,128)(2,1)S(1)}, u32[]{:S(2)}, u32[]{:S(2)}) collective-permute-start(bf16[16,8192]{1,0:T(8,128)(2,1)} %add_convert_fusion.2), channel_id=1, source_target_pairs={{32,0},{64,32},{96,64},{128,96},{160,128},{192,160},{224,192},{256... | collective-permute-start | bytes 786440 | tf_op jit(solution)/shard_map/while/body/eval_jaxpr/ppermute | solution.py:13
  374.9 8.5 %collective-permute-start = (bf16[16,8192]{1,0:T(8,128)(2,1)}, bf16[16,8192]{1,0:T(8,128)(2,1)S(1)}, u32[]{:S(2)}, u32[]{:S(2)}) collective-permute-start(bf16[16,8192]{1,0:T(8,128)(2,1)} %add_convert_fusion.2), channel_id=1, source_target_pairs={{32,0},{64,32},{96,64},{128,96},{160,128},{192,160},{224,192},{256... | collective-permute-start | bytes 786440 | tf_op jit(solution)/shard_map/while/body/eval_jaxpr/ppermute | solution.py:13
  388.4 8.5 %collective-permute-start = (bf16[16,8192]{1,0:T(8,128)(2,1)}, bf16[16,8192]{1,0:T(8,128)(2,1)S(1)}, u32[]{:S(2)}, u32[]{:S(2)}) collective-permute-start(bf16[16,8192]{1,0:T(8,128)(2,1)} %add_convert_fusion.2), channel_id=1, source_target_pairs={{32,0},{64,32},{96,64},{128,96},{160,128},{192,160},{224,192},{256... | collective-permute-start | bytes 786440 | tf_op jit(solution)/shard_map/while/body/eval_jaxpr/ppermute | solution.py:13
  410.5 174.8 %all-gather.7.cloned.1.call-start = ((), (), s32[]{:S(2)}) async-start(), calls=%async_computation.3 | async-start | bytes 1474560 | tf_op jit(solution)/shard_map/all_gather | solution.py:97
  (10 other events, 31.0 us)
Sparse Core Ops, SparseCore 0:
  11.0 63.9 all-gather.4
  410.7 65.7 reduce-scatter.1
  478.6 31.4 all-gather.6
where the time goes:
time: 597 us; the launch traced here: 594 us
  waiting for transfers between devices  306 us (51%)
  blocking collectives  106 us (18%)
  other arithmetic  75.5 us (13%)
  matrix products  54.4 us (9%)
  starting transfers between devices  29.6 us (5%)
  between operations  13.9 us (2%)
  local copies, waits for them, and re-layouts  8.42 us (1%)
    ppermute x23, waiting for transfers between devices, from_behind(): lax.ppermute(value, axis, [(source, source + steps) for source in range(i...  176 us
    psum x1, blocking collectives, on_device(): totals = lax.psum(squares, ('pipe', 'seq', 'dp'))  106 us
    reduce_scatter x1, waiting for transfers between devices, on_device(): part = lax.psum_scatter(grads, 'seq', scatter_dimension=1, tiled=True)  65.9 us
    all_gather x1, waiting for transfers between devices, on_device(): whole = lax.all_gather(params, ('seq', 'dp'), axis=1, tiled=True)  64.3 us
    dot_general x23, matrix products, back_block(): jnp.dot(d_low, a_full, preferred_element_type=jnp.float32)  44.9 us
    convert_element_type x23, other arithmetic, back_block(): return hidden_gradient.astype(jnp.bfloat16)  42.7 us
    ppermute x23, starting transfers between devices, from_behind(): lax.ppermute(value, axis, [(source, source + steps) for source in range(i...  29.4 us
    dynamic_update_slice x23, other arithmetic, turn(): store = lax.dynamic_update_slice_in_dim(store, source[None], slot, 0)  23.3 us
  transfers between devices with their start and end apart: 26, of which 25 were waited for; matrix products, arithmetic and copies ran while one was open for 1% of the time, Pallas kernels for 0%

commit v1 on v0

--- a/solution.py
+++ b/solution.py
@@ -20,7 +20,10 @@
     top = top_grad[0]
     rank = a_rows.shape[1]
     params = jnp.concatenate([a_rows[0], b_rows[0], gain], axis=0)
-    whole = lax.all_gather(params, ("seq", "dp"), axis=1, tiled=True)
+    whole = jnp.concatenate(
+        lax.all_to_all(jnp.stack([params] * lax.axis_size(("seq", "dp"))), ("seq", "dp"), 0, 0),
+        axis=1,
+    )
     a_full = whole[:rank]
     b_full = whole[rank : 2 * rank]
     gain_float = whole[2 * rank].astype(jnp.float32)

time: 597 us -> 561 us (0.940)
  waiting for transfers between devices: 306 us -> 260 us
  starting transfers between devices: 29.6 us -> 40.6 us
    all_gather x1 -> x0, waiting for transfers between devices: 64.3 us -> none  [on_device(): whole = lax.all_gather(params, ('seq', 'dp'), axis=1, tiled=True)]
    all_to_all x0 -> x1, waiting for transfers between devices: none -> 16.9 us  [on_device(): lax.all_to_all(jnp.stack([params] * lax.axis_size(('seq', 'dp'))), ('seq'...]
    all_to_all x0 -> x1, starting transfers between devices: none -> 11.1 us  [on_device(): lax.all_to_all(jnp.stack([params] * lax.axis_size(('seq', 'dp'))), ('seq'...]
where the time goes in v1:
time: 561 us; the launch traced here: 558 us
  waiting for transfers between devices  260 us (46%)
  blocking collectives  106 us (19%)
  other arithmetic  74.8 us (13%)
  matrix products  52.6 us (9%)
  starting transfers between devices  40.6 us (7%)
  between operations  14.2 us (3%)
  local copies, waits for them, and re-layouts  9.58 us (2%)
    ppermute x23, waiting for transfers between devices, from_behind(): lax.ppermute(value, axis, [(source, source + steps) for source in range(i...  172 us
    psum x1, blocking collectives, on_device(): totals = lax.psum(squares, ('pipe', 'seq', 'dp'))  106 us
    reduce_scatter x1, waiting for transfers between devices, on_device(): part = lax.psum_scatter(grads, 'seq', scatter_dimension=1, tiled=True)  70.7 us
    dot_general x23, matrix products, back_block(): jnp.dot(d_low, a_full, preferred_element_type=jnp.float32)  44.9 us
    convert_element_type x23, other arithmetic, back_block(): return hidden_gradient.astype(jnp.bfloat16)  42.6 us
    ppermute x23, starting transfers between devices, from_behind(): lax.ppermute(value, axis, [(source, source + steps) for source in range(i...  29.4 us
    dynamic_update_slice x23, other arithmetic, turn(): store = lax.dynamic_update_slice_in_dim(store, source[None], slot, 0)  23.3 us
    all_to_all x1, waiting for transfers between devices, on_device(): lax.all_to_all(jnp.stack([params] * lax.axis_size(('seq', 'dp'))), ('seq'...  16.9 us
  transfers between devices with their start and end apart: 26, of which 25 were waited for; matrix products, arithmetic and copies ran while one was open for 1% of the time, Pallas kernels for 0%

profile of v1, /device:TPU:1, one launch (start us, length us, event | category | flops | bytes accessed | tf_op | source)
XLA Modules:
  0.0 558.2 jit_solution(3656288521073063373)
XLA Ops:
  9.2 11.1 %all-to-all-start = ((bf16[32,65,256]{2,1,0:T(8,128)(2,1)}), bf16[32,65,256]{2,1,0:T(8,128)(2,1)}, u32[]{:S(2)}, u32[]{:S(2)}) async-start(bf16[32,65,256]{2,1,0:T(8,128)(2,1)} %stack.2), calls=%async_computation | async-start | bytes 2359296 | tf_op jit(solution)/shard_map/all_to_all | solution.py:24
  20.9 16.9 %all-to-all-done = bf16[32,65,256]{2,1,0:T(8,128)(2,1)} async-done(((bf16[32,65,256]{2,1,0:T(8,128)(2,1)}), bf16[32,65,256]{2,1,0:T(8,128)(2,1)}, u32[]{:S(2)}, u32[]{:S(2)}) %all-to-all-start) | async-done | bytes 1064992 | tf_op jit(solution)/shard_map/all_to_all | solution.py:24
  41.9 314.9 %while.17 = (s32[]{:T(128)}, bf16[16,8192]{1,0:T(8,128)(2,1)S(1)}, bf16[9,16,8192]{2,1,0:T(8,128)(2,1)S(1)}, pred[]{:T(512)}, s32[]{:T(128)}, /*index=5*/bf16[12...) while((s32[]{:T(128)}, bf16[16,8192]{1,0:T(8,128)(2,1)S(1)}, ...), condition=%wide.region_3.4_spmd, body=%wide.region_1.3_spmd.sunk | while | flops 18612752 | bytes 5538680 | solution.py:80
  48.2 7.4 %collective-permute-done = bf16[16,8192]{1,0:T(8,128)(2,1)S(1)} collective-permute-done((bf16[16,8192]{1,0:T(8,128)(2,1)}, bf16[16,8192]{1,0:T(8,128)(2,1)S(1)}, u32[]{:S(2)}, u32[]{:S(2)}) %collective-permute-start) | collective-permute-done | bytes 262176 | tf_op jit(solution)/shard_map/while/body/eval_jaxpr/ppermute | solution.py:13
  86.7 6.6 %collective-permute-done = bf16[16,8192]{1,0:T(8,128)(2,1)S(1)} collective-permute-done((bf16[16,8192]{1,0:T(8,128)(2,1)}, bf16[16,8192]{1,0:T(8,128)(2,1)S(1)}, u32[]{:S(2)}, u32[]{:S(2)}) %collective-permute-start) | collective-permute-done | bytes 262176 | tf_op jit(solution)/shard_map/while/body/eval_jaxpr/ppermute | solution.py:13
  112.2 7.2 %collective-permute-done = bf16[16,8192]{1,0:T(8,128)(2,1)S(1)} collective-permute-done((bf16[16,8192]{1,0:T(8,128)(2,1)}, bf16[16,8192]{1,0:T(8,128)(2,1)S(1)}, u32[]{:S(2)}, u32[]{:S(2)}) %collective-permute-start) | collective-permute-done | bytes 262176 | tf_op jit(solution)/shard_map/while/body/eval_jaxpr/ppermute | solution.py:13
  125.6 7.2 %collective-permute-done = bf16[16,8192]{1,0:T(8,128)(2,1)S(1)} collective-permute-done((bf16[16,8192]{1,0:T(8,128)(2,1)}, bf16[16,8192]{1,0:T(8,128)(2,1)S(1)}, u32[]{:S(2)}, u32[]{:S(2)}) %collective-permute-start) | collective-permute-done | bytes 262176 | tf_op jit(solution)/shard_map/while/body/eval_jaxpr/ppermute | solution.py:13
  139.0 7.2 %collective-permute-done = bf16[16,8192]{1,0:T(8,128)(2,1)S(1)} collective-permute-done((bf16[16,8192]{1,0:T(8,128)(2,1)}, bf16[16,8192]{1,0:T(8,128)(2,1)S(1)}, u32[]{:S(2)}, u32[]{:S(2)}) %collective-permute-start) | collective-permute-done | bytes 262176 | tf_op jit(solution)/shard_map/while/body/eval_jaxpr/ppermute | solution.py:13
  152.5 7.2 %collective-permute-done = bf16[16,8192]{1,0:T(8,128)(2,1)S(1)} collective-permute-done((bf16[16,8192]{1,0:T(8,128)(2,1)}, bf16[16,8192]{1,0:T(8,128)(2,1)S(1)}, u32[]{:S(2)}, u32[]{:S(2)}) %collective-permute-start) | collective-permute-done | bytes 262176 | tf_op jit(solution)/shard_map/while/body/eval_jaxpr/ppermute | solution.py:13
  165.9 7.2 %collective-permute-done = bf16[16,8192]{1,0:T(8,128)(2,1)S(1)} collective-permute-done((bf16[16,8192]{1,0:T(8,128)(2,1)}, bf16[16,8192]{1,0:T(8,128)(2,1)S(1)}, u32[]{:S(2)}, u32[]{:S(2)}) %collective-permute-start) | collective-permute-done | bytes 262176 | tf_op jit(solution)/shard_map/while/body/eval_jaxpr/ppermute | solution.py:13
  179.3 7.2 %collective-permute-done = bf16[16,8192]{1,0:T(8,128)(2,1)S(1)} collective-permute-done((bf16[16,8192]{1,0:T(8,128)(2,1)}, bf16[16,8192]{1,0:T(8,128)(2,1)S(1)}, u32[]{:S(2)}, u32[]{:S(2)}) %collective-permute-start) | collective-permute-done | bytes 262176 | tf_op jit(solution)/shard_map/while/body/eval_jaxpr/ppermute | solution.py:13
  192.8 8.3 %collective-permute-done = bf16[16,8192]{1,0:T(8,128)(2,1)S(1)} collective-permute-done((bf16[16,8192]{1,0:T(8,128)(2,1)}, bf16[16,8192]{1,0:T(8,128)(2,1)S(1)}, u32[]{:S(2)}, u32[]{:S(2)}) %collective-permute-start) | collective-permute-done | bytes 262176 | tf_op jit(solution)/shard_map/while/body/eval_jaxpr/ppermute | solution.py:13
  207.3 9.9 %collective-permute-done = bf16[16,8192]{1,0:T(8,128)(2,1)S(1)} collective-permute-done((bf16[16,8192]{1,0:T(8,128)(2,1)}, bf16[16,8192]{1,0:T(8,128)(2,1)S(1)}, u32[]{:S(2)}, u32[]{:S(2)}) %collective-permute-start) | collective-permute-done | bytes 262176 | tf_op jit(solution)/shard_map/while/body/eval_jaxpr/ppermute | solution.py:13
  223.4 10.7 %collective-permute-done = bf16[16,8192]{1,0:T(8,128)(2,1)S(1)} collective-permute-done((bf16[16,8192]{1,0:T(8,128)(2,1)}, bf16[16,8192]{1,0:T(8,128)(2,1)S(1)}, u32[]{:S(2)}, u32[]{:S(2)}) %collective-permute-start) | collective-permute-done | bytes 262176 | tf_op jit(solution)/shard_map/while/body/eval_jaxpr/ppermute | solution.py:13
  240.3 9.8 %collective-permute-done = bf16[16,8192]{1,0:T(8,128)(2,1)S(1)} collective-permute-done((bf16[16,8192]{1,0:T(8,128)(2,1)}, bf16[16,8192]{1,0:T(8,128)(2,1)S(1)}, u32[]{:S(2)}, u32[]{:S(2)}) %collective-permute-start) | collective-permute-done | bytes 262176 | tf_op jit(solution)/shard_map/while/body/eval_jaxpr/ppermute | solution.py:13
  256.3 8.3 %collective-permute-done = bf16[16,8192]{1,0:T(8,128)(2,1)S(1)} collective-permute-done((bf16[16,8192]{1,0:T(8,128)(2,1)}, bf16[16,8192]{1,0:T(8,128)(2,1)S(1)}, u32[]{:S(2)}, u32[]{:S(2)}) %collective-permute-start) | collective-permute-done | bytes 262176 | tf_op jit(solution)/shard_map/while/body/eval_jaxpr/ppermute | solution.py:13
  270.7 6.8 %collective-permute-done = bf16[16,8192]{1,0:T(8,128)(2,1)S(1)} collective-permute-done((bf16[16,8192]{1,0:T(8,128)(2,1)}, bf16[16,8192]{1,0:T(8,128)(2,1)S(1)}, u32[]{:S(2)}, u32[]{:S(2)}) %collective-permute-start) | collective-permute-done | bytes 262176 | tf_op jit(solution)/shard_map/while/body/eval_jaxpr/ppermute | solution.py:13
  296.2 7.0 %collective-permute-done = bf16[16,8192]{1,0:T(8,128)(2,1)S(1)} collective-permute-done((bf16[16,8192]{1,0:T(8,128)(2,1)}, bf16[16,8192]{1,0:T(8,128)(2,1)S(1)}, u32[]{:S(2)}, u32[]{:S(2)}) %collective-permute-start) | collective-permute-done | bytes 262176 | tf_op jit(solution)/shard_map/while/body/eval_jaxpr/ppermute | solution.py:13
  309.3 7.2 %collective-permute-done = bf16[16,8192]{1,0:T(8,128)(2,1)S(1)} collective-permute-done((bf16[16,8192]{1,0:T(8,128)(2,1)}, bf16[16,8192]{1,0:T(8,128)(2,1)S(1)}, u32[]{:S(2)}, u32[]{:S(2)}) %collective-permute-start) | collective-permute-done | bytes 262176 | tf_op jit(solution)/shard_map/while/body/eval_jaxpr/ppermute | solution.py:13
  322.8 7.2 %collective-permute-done = bf16[16,8192]{1,0:T(8,128)(2,1)S(1)} collective-permute-done((bf16[16,8192]{1,0:T(8,128)(2,1)}, bf16[16,8192]{1,0:T(8,128)(2,1)S(1)}, u32[]{:S(2)}, u32[]{:S(2)}) %collective-permute-start) | collective-permute-done | bytes 262176 | tf_op jit(solution)/shard_map/while/body/eval_jaxpr/ppermute | solution.py:13
  336.2 7.2 %collective-permute-done = bf16[16,8192]{1,0:T(8,128)(2,1)S(1)} collective-permute-done((bf16[16,8192]{1,0:T(8,128)(2,1)}, bf16[16,8192]{1,0:T(8,128)(2,1)S(1)}, u32[]{:S(2)}, u32[]{:S(2)}) %collective-permute-start) | collective-permute-done | bytes 262176 | tf_op jit(solution)/shard_map/while/body/eval_jaxpr/ppermute | solution.py:13
  349.6 7.2 %collective-permute-done = bf16[16,8192]{1,0:T(8,128)(2,1)S(1)} collective-permute-done((bf16[16,8192]{1,0:T(8,128)(2,1)}, bf16[16,8192]{1,0:T(8,128)(2,1)S(1)}, u32[]{:S(2)}, u32[]{:S(2)}) %collective-permute-start) | collective-permute-done | bytes 262176 | tf_op jit(solution)/shard_map/while/body/eval_jaxpr/ppermute | solution.py:13
  369.6 70.7 %reduce-scatter.2.cloned.1.call-done = f32[65,1024]{1,0:T(8,128)} async-done(((f32[65,8192]{1,0:T(8,128)}), f32[65,1024]{1,0:T(8,128)}) %reduce-scatter.2.cloned.1.call-update) | async-done | bytes 266256 | tf_op jit(solution)/shard_map/reduce_scatter | solution.py:92
  442.6 105.9 %psum.7 = f32[4]{0:T(128)S(1)} all-reduce(f32[4]{0:T(128)S(1)} %compare_select_fusion), channel_id=1, replica_groups=mesh['pipe'=16,'seq'=8,'dp'=4] {'pipe','seq','dp'}, use_global_device_ids=true, to_apply=%region_7.8 | all-reduce | flops 4 | bytes 32 | tf_op jit(solution)/shard_map/psum | solution.py:97
  (180 shorter events, 192.0 us)
Async XLA Ops:
  9.2 28.6 %all-to-all-start = ((bf16[32,65,256]{2,1,0:T(8,128)(2,1)}), bf16[32,65,256]{2,1,0:T(8,128)(2,1)}, u32[]{:S(2)}, u32[]{:S(2)}) async-start(bf16[32,65,256]{2,1,0:T(8,128)(2,1)} %stack.2), calls=%async_computation | async-start | bytes 2359296 | tf_op jit(solution)/shard_map/all_to_all | solution.py:24
  20.3 420.0 %reduce-scatter.2.cloned.1.call-start = ((), (), s32[]{:S(2)}) async-start(), calls=%async_computation.2 | async-start | bytes 2654208 | tf_op jit(solution)/shard_map/reduce_scatter | solution.py:92
  46.9 8.7 %collective-permute-start = (bf16[16,8192]{1,0:T(8,128)(2,1)}, bf16[16,8192]{1,0:T(8,128)(2,1)S(1)}, u32[]{:S(2)}, u32[]{:S(2)}) collective-permute-start(bf16[16,8192]{1,0:T(8,128)(2,1)} %add_convert_fusion.2), channel_id=1, source_target_pairs={{32,0},{64,32},{96,64},{128,96},{160,128},{192,160},{224,192},{256... | collective-permute-start | bytes 786440 | tf_op jit(solution)/shard_map/while/body/eval_jaxpr/ppermute | solution.py:13
  60.5 7.8 %collective-permute-start = (bf16[16,8192]{1,0:T(8,128)(2,1)}, bf16[16,8192]{1,0:T(8,128)(2,1)S(1)}, u32[]{:S(2)}, u32[]{:S(2)}) collective-permute-start(bf16[16,8192]{1,0:T(8,128)(2,1)} %add_convert_fusion.2), channel_id=1, source_target_pairs={{32,0},{64,32},{96,64},{128,96},{160,128},{192,160},{224,192},{256... | collective-permute-start | bytes 786440 | tf_op jit(solution)/shard_map/while/body/eval_jaxpr/ppermute | solution.py:13
  85.4 7.8 %collective-permute-start = (bf16[16,8192]{1,0:T(8,128)(2,1)}, bf16[16,8192]{1,0:T(8,128)(2,1)S(1)}, u32[]{:S(2)}, u32[]{:S(2)}) collective-permute-start(bf16[16,8192]{1,0:T(8,128)(2,1)} %add_convert_fusion.2), channel_id=1, source_target_pairs={{32,0},{64,32},{96,64},{128,96},{160,128},{192,160},{224,192},{256... | collective-permute-start | bytes 786440 | tf_op jit(solution)/shard_map/while/body/eval_jaxpr/ppermute | solution.py:13
  98.2 7.8 %collective-permute-start = (bf16[16,8192]{1,0:T(8,128)(2,1)}, bf16[16,8192]{1,0:T(8,128)(2,1)S(1)}, u32[]{:S(2)}, u32[]{:S(2)}) collective-permute-start(bf16[16,8192]{1,0:T(8,128)(2,1)} %add_convert_fusion.2), channel_id=1, source_target_pairs={{32,0},{64,32},{96,64},{128,96},{160,128},{192,160},{224,192},{256... | collective-permute-start | bytes 786440 | tf_op jit(solution)/shard_map/while/body/eval_jaxpr/ppermute | solution.py:13
  110.9 8.5 %collective-permute-start = (bf16[16,8192]{1,0:T(8,128)(2,1)}, bf16[16,8192]{1,0:T(8,128)(2,1)S(1)}, u32[]{:S(2)}, u32[]{:S(2)}) collective-permute-start(bf16[16,8192]{1,0:T(8,128)(2,1)} %add_convert_fusion.2), channel_id=1, source_target_pairs={{32,0},{64,32},{96,64},{128,96},{160,128},{192,160},{224,192},{256... | collective-permute-start | bytes 786440 | tf_op jit(solution)/shard_map/while/body/eval_jaxpr/ppermute | solution.py:13
  124.3 8.5 %collective-permute-start = (bf16[16,8192]{1,0:T(8,128)(2,1)}, bf16[16,8192]{1,0:T(8,128)(2,1)S(1)}, u32[]{:S(2)}, u32[]{:S(2)}) collective-permute-start(bf16[16,8192]{1,0:T(8,128)(2,1)} %add_convert_fusion.2), channel_id=1, source_target_pairs={{32,0},{64,32},{96,64},{128,96},{160,128},{192,160},{224,192},{256... | collective-permute-start | bytes 786440 | tf_op jit(solution)/shard_map/while/body/eval_jaxpr/ppermute | solution.py:13
  137.8 8.5 %collective-permute-start = (bf16[16,8192]{1,0:T(8,128)(2,1)}, bf16[16,8192]{1,0:T(8,128)(2,1)S(1)}, u32[]{:S(2)}, u32[]{:S(2)}) collective-permute-start(bf16[16,8192]{1,0:T(8,128)(2,1)} %add_convert_fusion.2), channel_id=1, source_target_pairs={{32,0},{64,32},{96,64},{128,96},{160,128},{192,160},{224,192},{256... | collective-permute-start | bytes 786440 | tf_op jit(solution)/shard_map/while/body/eval_jaxpr/ppermute | solution.py:13
  151.2 8.5 %collective-permute-start = (bf16[16,8192]{1,0:T(8,128)(2,1)}, bf16[16,8192]{1,0:T(8,128)(2,1)S(1)}, u32[]{:S(2)}, u32[]{:S(2)}) collective-permute-start(bf16[16,8192]{1,0:T(8,128)(2,1)} %add_convert_fusion.2), channel_id=1, source_target_pairs={{32,0},{64,32},{96,64},{128,96},{160,128},{192,160},{224,192},{256... | collective-permute-start | bytes 786440 | tf_op jit(solution)/shard_map/while/body/eval_jaxpr/ppermute | solution.py:13
  164.6 8.5 %collective-permute-start = (bf16[16,8192]{1,0:T(8,128)(2,1)}, bf16[16,8192]{1,0:T(8,128)(2,1)S(1)}, u32[]{:S(2)}, u32[]{:S(2)}) collective-permute-start(bf16[16,8192]{1,0:T(8,128)(2,1)} %add_convert_fusion.2), channel_id=1, source_target_pairs={{32,0},{64,32},{96,64},{128,96},{160,128},{192,160},{224,192},{256... | collective-permute-start | bytes 786440 | tf_op jit(solution)/shard_map/while/body/eval_jaxpr/ppermute | solution.py:13
  178.0 8.5 %collective-permute-start = (bf16[16,8192]{1,0:T(8,128)(2,1)}, bf16[16,8192]{1,0:T(8,128)(2,1)S(1)}, u32[]{:S(2)}, u32[]{:S(2)}) collective-permute-start(bf16[16,8192]{1,0:T(8,128)(2,1)} %add_convert_fusion.2), channel_id=1, source_target_pairs={{32,0},{64,32},{96,64},{128,96},{160,128},{192,160},{224,192},{256... | collective-permute-start | bytes 786440 | tf_op jit(solution)/shard_map/while/body/eval_jaxpr/ppermute | solution.py:13
  191.5 9.6 %collective-permute-start = (bf16[16,8192]{1,0:T(8,128)(2,1)}, bf16[16,8192]{1,0:T(8,128)(2,1)S(1)}, u32[]{:S(2)}, u32[]{:S(2)}) collective-permute-start(bf16[16,8192]{1,0:T(8,128)(2,1)} %add_convert_fusion.2), channel_id=1, source_target_pairs={{32,0},{64,32},{96,64},{128,96},{160,128},{192,160},{224,192},{256... | collective-permute-start | bytes 786440 | tf_op jit(solution)/shard_map/while/body/eval_jaxpr/ppermute | solution.py:13
  206.0 11.2 %collective-permute-start = (bf16[16,8192]{1,0:T(8,128)(2,1)}, bf16[16,8192]{1,0:T(8,128)(2,1)S(1)}, u32[]{:S(2)}, u32[]{:S(2)}) collective-permute-start(bf16[16,8192]{1,0:T(8,128)(2,1)} %add_convert_fusion.2), channel_id=1, source_target_pairs={{32,0},{64,32},{96,64},{128,96},{160,128},{192,160},{224,192},{256... | collective-permute-start | bytes 786440 | tf_op jit(solution)/shard_map/while/body/eval_jaxpr/ppermute | solution.py:13
  222.1 12.0 %collective-permute-start = (bf16[16,8192]{1,0:T(8,128)(2,1)}, bf16[16,8192]{1,0:T(8,128)(2,1)S(1)}, u32[]{:S(2)}, u32[]{:S(2)}) collective-permute-start(bf16[16,8192]{1,0:T(8,128)(2,1)} %add_convert_fusion.2), channel_id=1, source_target_pairs={{32,0},{64,32},{96,64},{128,96},{160,128},{192,160},{224,192},{256... | collective-permute-start | bytes 786440 | tf_op jit(solution)/shard_map/while/body/eval_jaxpr/ppermute | solution.py:13
  239.0 11.1 %collective-permute-start = (bf16[16,8192]{1,0:T(8,128)(2,1)}, bf16[16,8192]{1,0:T(8,128)(2,1)S(1)}, u32[]{:S(2)}, u32[]{:S(2)}) collective-permute-start(bf16[16,8192]{1,0:T(8,128)(2,1)} %add_convert_fusion.2), channel_id=1, source_target_pairs={{32,0},{64,32},{96,64},{128,96},{160,128},{192,160},{224,192},{256... | collective-permute-start | bytes 786440 | tf_op jit(solution)/shard_map/while/body/eval_jaxpr/ppermute | solution.py:13
  255.0 9.6 %collective-permute-start = (bf16[16,8192]{1,0:T(8,128)(2,1)}, bf16[16,8192]{1,0:T(8,128)(2,1)S(1)}, u32[]{:S(2)}, u32[]{:S(2)}) collective-permute-start(bf16[16,8192]{1,0:T(8,128)(2,1)} %add_convert_fusion.2), channel_id=1, source_target_pairs={{32,0},{64,32},{96,64},{128,96},{160,128},{192,160},{224,192},{256... | collective-permute-start | bytes 786440 | tf_op jit(solution)/shard_map/while/body/eval_jaxpr/ppermute | solution.py:13
  269.4 8.1 %collective-permute-start = (bf16[16,8192]{1,0:T(8,128)(2,1)}, bf16[16,8192]{1,0:T(8,128)(2,1)S(1)}, u32[]{:S(2)}, u32[]{:S(2)}) collective-permute-start(bf16[16,8192]{1,0:T(8,128)(2,1)} %add_convert_fusion.2), channel_id=1, source_target_pairs={{32,0},{64,32},{96,64},{128,96},{160,128},{192,160},{224,192},{256... | collective-permute-start | bytes 786440 | tf_op jit(solution)/shard_map/while/body/eval_jaxpr/ppermute | solution.py:13
  294.9 8.2 %collective-permute-start = (bf16[16,8192]{1,0:T(8,128)(2,1)}, bf16[16,8192]{1,0:T(8,128)(2,1)S(1)}, u32[]{:S(2)}, u32[]{:S(2)}) collective-permute-start(bf16[16,8192]{1,0:T(8,128)(2,1)} %add_convert_fusion.2), channel_id=1, source_target_pairs={{32,0},{64,32},{96,64},{128,96},{160,128},{192,160},{224,192},{256... | collective-permute-start | bytes 786440 | tf_op jit(solution)/shard_map/while/body/eval_jaxpr/ppermute | solution.py:13
  308.1 8.5 %collective-permute-start = (bf16[16,8192]{1,0:T(8,128)(2,1)}, bf16[16,8192]{1,0:T(8,128)(2,1)S(1)}, u32[]{:S(2)}, u32[]{:S(2)}) collective-permute-start(bf16[16,8192]{1,0:T(8,128)(2,1)} %add_convert_fusion.2), channel_id=1, source_target_pairs={{32,0},{64,32},{96,64},{128,96},{160,128},{192,160},{224,192},{256... | collective-permute-start | bytes 786440 | tf_op jit(solution)/shard_map/while/body/eval_jaxpr/ppermute | solution.py:13
  321.5 8.5 %collective-permute-start = (bf16[16,8192]{1,0:T(8,128)(2,1)}, bf16[16,8192]{1,0:T(8,128)(2,1)S(1)}, u32[]{:S(2)}, u32[]{:S(2)}) collective-permute-start(bf16[16,8192]{1,0:T(8,128)(2,1)} %add_convert_fusion.2), channel_id=1, source_target_pairs={{32,0},{64,32},{96,64},{128,96},{160,128},{192,160},{224,192},{256... | collective-permute-start | bytes 786440 | tf_op jit(solution)/shard_map/while/body/eval_jaxpr/ppermute | solution.py:13
  334.9 8.5 %collective-permute-start = (bf16[16,8192]{1,0:T(8,128)(2,1)}, bf16[16,8192]{1,0:T(8,128)(2,1)S(1)}, u32[]{:S(2)}, u32[]{:S(2)}) collective-permute-start(bf16[16,8192]{1,0:T(8,128)(2,1)} %add_convert_fusion.2), channel_id=1, source_target_pairs={{32,0},{64,32},{96,64},{128,96},{160,128},{192,160},{224,192},{256... | collective-permute-start | bytes 786440 | tf_op jit(solution)/shard_map/while/body/eval_jaxpr/ppermute | solution.py:13
  348.3 8.5 %collective-permute-start = (bf16[16,8192]{1,0:T(8,128)(2,1)}, bf16[16,8192]{1,0:T(8,128)(2,1)S(1)}, u32[]{:S(2)}, u32[]{:S(2)}) collective-permute-start(bf16[16,8192]{1,0:T(8,128)(2,1)} %add_convert_fusion.2), channel_id=1, source_target_pairs={{32,0},{64,32},{96,64},{128,96},{160,128},{192,160},{224,192},{256... | collective-permute-start | bytes 786440 | tf_op jit(solution)/shard_map/while/body/eval_jaxpr/ppermute | solution.py:13
  369.6 179.5 %all-gather.4.cloned.1.call-start = ((), (), s32[]{:S(2)}) async-start(), calls=%async_computation.3 | async-start | bytes 1474560 | tf_op jit(solution)/shard_map/all_gather | solution.py:100
  (7 other events, 37.3 us)
Sparse Core Ops, SparseCore 0:
  369.7 70.5 reduce-scatter.1
  442.4 31.2 all-gather.3
